TPU v7x, 512 devices: a whole 4x8x8 slice. The times are simulated.
512 devices in a mesh: seg: 16 (over z, x_lo), tok: 32 (over x_hi, y, core).
Axes of the slice: x: 4 (x_hi: 2, x_lo: 2; x = x_hi * 2 + x_lo), y: 8, z: 8, core: 2. Of those that a mesh axis runs over, the one named last changes fastest.
Arguments:
- seg_queries: bfloat16 [16, 4096, 2048], P('seg', 'tok'), may hold values from -8 to 8
- seg_keys: bfloat16 [16, 4096, 512], P('seg', 'tok'), may hold values from -8 to 8
- seg_values: bfloat16 [16, 4096, 512], P('seg', 'tok'), may hold values from -8 to 8
- grad_out: bfloat16 [16, 4096, 2048], P('seg', 'tok'), may hold values from -6 to 6
- mem_init: float32 [256, 1024], P('tok'), may hold values from -6 to 6
- mem_query: bfloat16 [256, 512], P('tok'), may hold values from -8 to 8
- retention: float32 [16, 1024], P('seg'), may hold values from 0 to 1
- seg_len: int32 [16], replicated, may hold values from 1024 to 4096, as said below
- doc_start: int32 [16], replicated, may hold values from 0 to 1, as said below
Outputs:
- attended: bfloat16 [16, 4096, 2048], P('seg', 'tok')
- memory_in: float32 [16, 256, 1024], P('seg', 'tok')
- memory_grad: float32 [16, 256, 1024], P('seg', 'tok')
Inputs may be any that keep to these rules, and one draw needn't show every extreme that they name: `seg_len`: A segment is full unless it is the last one of its document; segment 0 is always full and the last segment is the last one of its document. `doc_start`: segment 0 begins a document and segment 1 never does; any later segment may.
All inputs are finite; a program needn't handle non-finite values.
Results may differ from a plain program's by a relative error of at most 0.009.
Values may be sent and summed in bfloat16 or wider, within the bound.
No kernel may reach another device: no remote copies, remote signals or barrier semaphores. Data moves between devices by JAX's collectives and lax.ppermute only.
A program may use at most 64 MiB of HBM per device.

v0:
```python
import math
import jax
import jax.numpy as jnp
from jax import lax
from jax.sharding import PartitionSpec as P

HD = 128
QH = 16
KVH = 4
loss_scale = 16.0
neg_fill = -1e30
norm_eps = 1e-06


def gathered(block, axis, groups):
    size = lax.axis_size(axis)
    index = lax.axis_index(axis)
    held = block[None]
    axis_bits = []
    for group in groups:
        group = sorted(group)
        mine = sum(((index >> bit & 1) << k for k, bit in enumerate(group)))
        arrived = [held]
        for mask in range(1, 1 << len(group)):
            flip = sum(((mask >> k & 1) << bit for k, bit in enumerate(group)))
            arrived.append(lax.ppermute(held, axis, [(i, i ^ flip) for i in range(size)]))
        placed = []
        for place in range(1 << len(group)):
            value = arrived[0]
            for mask in range(1, 1 << len(group)):
                value = jnp.where(mine ^ mask == place, arrived[mask], value)
            placed.append(value)
        held = jnp.stack(placed).reshape((2,) * len(group) + held.shape)
        axis_bits = group[::-1] + axis_bits
    order = sorted(range(len(axis_bits)), key=lambda k: -axis_bits[k])
    held = jnp.transpose(held, order + list(range(len(axis_bits), held.ndim)))
    return held.reshape((size,) + block.shape)


def scattered_sum(rows, axis, groups):
    size = lax.axis_size(axis)
    index = lax.axis_index(axis)
    held = rows.reshape((size, rows.shape[0] // size) + rows.shape[1:])
    low = 0
    for width in groups:
        ways = 1 << width
        held = held.reshape((held.shape[0] // ways, ways) + held.shape[1:])
        mine = index >> low & ways - 1
        total = lax.dynamic_index_in_dim(held, mine, axis=1, keepdims=False)
        for mask in range(1, ways):
            send = lax.dynamic_index_in_dim(held, mine ^ mask, axis=1, keepdims=False)
            flip = mask << low
            total = total + lax.ppermute(send, axis, [(i, i ^ flip) for i in range(size)])
        held = total
        low += width
    return held[0]


def slot_norm(raw_rows):
    parts = raw_rows.reshape(raw_rows.shape[0], 2 * KVH, HD)
    multiplier = lax.rsqrt(jnp.mean(parts * parts, axis=-1, keepdims=True) + norm_eps)
    return (parts * multiplier).reshape(raw_rows.shape)


def softmax_step(row_top, row_total, scores, allowed):
    scores = jnp.where(allowed, scores, neg_fill)
    new_top = jnp.maximum(row_top, jnp.max(scores, axis=-1))
    weights = jnp.where(allowed, jnp.exp(scores - new_top[..., None]), 0.0)
    multiplier = jnp.exp(row_top - new_top)
    new_total = row_total * multiplier + jnp.sum(weights, axis=-1)
    return (new_top, new_total, weights.astype(jnp.bfloat16), multiplier)


def shards(
    seg_queries, seg_keys, seg_values, grad_out, mem_init, mem_query, retention, seg_len, doc_start
):
    tok_rows = seg_queries.shape[1]
    mem_rows = mem_query.shape[0]
    group_size = QH // KVH
    width_kv = KVH * HD
    seg_count = lax.axis_size("seg")
    seg_index = lax.axis_index("seg")
    tok_index = lax.axis_index("tok")
    length = seg_len[seg_index]
    score_scale = 1.0 / math.sqrt(HD)
    queries = seg_queries[0].reshape(tok_rows, KVH, group_size, HD)
    slot_queries = mem_query.reshape(mem_rows, KVH, HD)
    row_pos = tok_index * tok_rows + jnp.arange(tok_rows)
    kv_piece = lax.all_gather(
        jnp.concatenate([seg_keys[0], seg_values[0]], axis=1), "tok", axis=0, tiled=True
    )
    piece_rows = kv_piece.shape[0]
    key_piece = kv_piece[:, :width_kv].reshape(piece_rows, KVH, HD)
    value_piece = kv_piece[:, width_kv:].reshape(piece_rows, KVH, HD)
    live_keys = jnp.arange(piece_rows) < length
    slot_scores = (
        jnp.einsum("rgd,ugd->gru", slot_queries, key_piece, preferred_element_type=jnp.float32)
        * score_scale
    )
    slot_scores = jnp.where(live_keys, slot_scores, neg_fill)
    slot_top = jnp.max(slot_scores, axis=-1, keepdims=True)
    slot_exp = jnp.where(live_keys, jnp.exp(slot_scores - slot_top), 0.0)
    slot_denom = jnp.transpose(jnp.sum(slot_exp, axis=-1))[..., None]
    slot_weights = slot_exp.astype(jnp.bfloat16)
    slot_keys = jnp.einsum(
        "gru,ugd->rgd", slot_weights, key_piece, preferred_element_type=jnp.float32
    )
    slot_values = jnp.einsum(
        "gru,ugd->rgd", slot_weights, value_piece, preferred_element_type=jnp.float32
    )
    raw_slots = jnp.concatenate(
        [
            (slot_keys / slot_denom).reshape(mem_rows, width_kv),
            (slot_values / slot_denom).reshape(mem_rows, width_kv),
        ],
        axis=1,
    )
    written = slot_norm(raw_slots)
    ret_row = retention[0]
    following = doc_start[jnp.minimum(seg_index + 1, seg_count - 1)].astype(jnp.float32)
    keep_flag = jnp.where(seg_index == seg_count - 1, 1.0, 1.0 - following)
    decay_rate = keep_flag * ret_row
    carried = keep_flag * (1.0 - ret_row) * written + (1.0 - keep_flag) * mem_init
    chain_terms = gathered(
        jnp.concatenate([carried, decay_rate[None]], axis=0), "seg", ((2, 3), (0, 1))
    )
    all_carried = chain_terms[:, :mem_rows]
    all_decay = chain_terms[:, mem_rows]
    memory_in = mem_init
    for step in range(seg_count - 1):
        following_memory = all_decay[step] * memory_in + all_carried[step]
        memory_in = jnp.where(step < seg_index, following_memory, memory_in)
    block_rows = math.gcd(piece_rows, 1024)
    blocks = piece_rows // block_rows
    running = (
        jnp.full((KVH, group_size, tok_rows), neg_fill, jnp.float32),
        jnp.zeros((KVH, group_size, tok_rows), jnp.float32),
        jnp.zeros((tok_rows, KVH, group_size, HD), jnp.float32),
    )
    for block in range(blocks):
        block_start = block * block_rows
        key_block = key_piece[block_start : block_start + block_rows]
        value_block = value_piece[block_start : block_start + block_rows]
        columns = block_start + jnp.arange(block_rows)
        causal = (columns[None, :] <= row_pos[:, None]) & (columns < length)[None, :]
        seg_scores = (
            jnp.einsum("tgjd,ugd->gjtu", queries, key_block, preferred_element_type=jnp.float32)
            * score_scale
        )
        seg_top, seg_total, seg_weights, seg_factor = softmax_step(
            running[0], running[1], seg_scores, causal
        )
        seg_acc = running[2] * jnp.transpose(seg_factor, (2, 0, 1))[..., None] + jnp.einsum(
            "gjtu,ugd->tgjd", seg_weights, value_block, preferred_element_type=jnp.float32
        )
        running = (seg_top, seg_total, seg_acc)
    memory_all = gathered(memory_in.astype(jnp.bfloat16), "tok", ((3, 4), (1, 2), (0,))).reshape(
        -1, 2 * width_kv
    )
    mem_keys = memory_all[:, :width_kv].reshape(-1, KVH, HD)
    mem_vals = memory_all[:, width_kv:].reshape(-1, KVH, HD)
    mem_scores = (
        jnp.einsum("tgjd,mgd->gjtm", queries, mem_keys, preferred_element_type=jnp.float32)
        * score_scale
    )
    row_top = jnp.maximum(running[0], jnp.max(mem_scores, axis=-1))
    seg_factor = jnp.exp(running[0] - row_top)
    mem_weights = jnp.exp(mem_scores - row_top[..., None])
    row_total = running[1] * seg_factor + jnp.sum(mem_weights, axis=-1)
    weighted = running[2] * jnp.transpose(seg_factor, (2, 0, 1))[..., None] + jnp.einsum(
        "gjtm,mgd->tgjd",
        mem_weights.astype(jnp.bfloat16),
        mem_vals,
        preferred_element_type=jnp.float32,
    )
    att_rows = weighted / jnp.transpose(row_total, (2, 0, 1))[..., None]
    log_total = row_top + jnp.log(row_total)
    attended = att_rows.reshape(1, tok_rows, QH * HD).astype(jnp.bfloat16)
    valid_rows = (row_pos < length).astype(jnp.bfloat16)[:, None]
    cotangent = (grad_out[0] * valid_rows * loss_scale).reshape(tok_rows, KVH, group_size, HD)
    row_delta = jnp.einsum("tgjd,tgjd->gjt", cotangent.astype(jnp.float32), att_rows)
    mem_prob = jnp.exp(mem_scores - log_total[..., None])
    grad_prob = jnp.einsum(
        "tgjd,mgd->gjtm", cotangent, mem_vals, preferred_element_type=jnp.float32
    )
    grad_score = mem_prob * (grad_prob - row_delta[..., None])
    grad_vals = jnp.einsum(
        "gjtm,tgjd->mgd",
        mem_prob.astype(jnp.bfloat16),
        cotangent,
        preferred_element_type=jnp.float32,
    )
    grad_keys = (
        jnp.einsum(
            "gjtm,tgjd->mgd",
            grad_score.astype(jnp.bfloat16),
            queries,
            preferred_element_type=jnp.float32,
        )
        * score_scale
    )
    grad_slots = jnp.concatenate(
        [grad_keys.reshape(-1, width_kv), grad_vals.reshape(-1, width_kv)], axis=1
    )
    local_grad = scattered_sum(grad_slots, "tok", (1, 2, 2))
    all_local = gathered(local_grad, "seg", ((2, 3), (0, 1)))
    memory_grad = all_local[seg_count - 1]
    for step in range(seg_count - 2, -1, -1):
        earlier_grad = all_local[step] + all_decay[step] * memory_grad
        memory_grad = jnp.where(step >= seg_index, earlier_grad, memory_grad)
    return (attended, memory_in[None], memory_grad[None])


def solution(mesh):
    placed = (
        P("seg", "tok", None),
        P("seg", "tok", None),
        P("seg", "tok", None),
        P("seg", "tok", None),
        P("tok", None),
        P("tok", None),
        P("seg", None),
        P(),
        P(),
    )
    return jax.shard_map(
        shards,
        mesh=mesh,
        in_specs=placed,
        out_specs=(P("seg", "tok", None), P("seg", "tok", None), P("seg", "tok", None)),
        check_vma=False,
    )
```

profile of v0, /device:TPU:2, one launch (start us, length us, event | category | flops | bytes accessed | tf_op | source)
XLA Modules:
  0.0 347.7 jit_solution(11766808417356156304)
XLA Ops:
  20.0 2.2 compare_and_fusion.1
  22.1 106.7 %all-gather.2.cloned.1.call-done = bf16[4096,1024]{0,1:T(8,128)(2,1)} async-done(((bf16[128,1024]{0,1:T(8,128)(2,1)}), bf16[4096,1024]{0,1:T(8,128)(2,1)}) %all-gather.2.cloned.1.call-update) | async-done | bytes 8388624 | tf_op jit(solution)/shard_map/all_gather | solution.py:89
  128.8 6.1 %fusion.185 = (bf16[4096,512]{0,1:T(8,128)(2,1)}, bf16[4096,512]{0,1:T(8,128)(2,1)}) fusion(bf16[4096,1024]{0,1:T(8,128)(2,1)} %all-gather.2.cloned.1.call-done), kind=kLoop, calls=%fused_computation.282 | loop fusion | bytes 16777216 | tf_op jit(solution)/shard_map/slice | solution.py:93
  134.9 3.1 fusion.188
  138.0 3.5 %fusion.80 = f32[8,4,128]{2,0,1:T(8,128)S(1)} fusion(bf16[4096,4,128]{0,2,1:T(8,128)(2,1)} %bitcast.616, bf16[4,8,4096]{2,1,0:T(8,128)(2,1)S(1)} %get-tuple-element.90, f32[8,4]{0,1:T(4,128)S(1)} %bitcast.687), kind=kOutput, calls=%fused_computation.70 | convolution fusion | flops 33558528 | bytes 4472960 | tf_op jit(solution)/shard_map/gru,ugd->rgd/dot_general | solution.py:105
  141.6 3.5 %fusion.79 = f32[8,4,128]{2,0,1:T(8,128)S(1)} fusion(bf16[4096,4,128]{0,2,1:T(8,128)(2,1)} %bitcast.614, bf16[4,8,4096]{2,1,0:T(8,128)(2,1)S(1)} %get-tuple-element.90, f32[8,4]{0,1:T(4,128)S(1)} %bitcast.688), kind=kOutput, calls=%fused_computation.68 | convolution fusion | flops 33558528 | bytes 4472960 | tf_op jit(solution)/shard_map/gru,ugd->rgd/dot_general | solution.py:108
  145.3 6.6 %collective-permute-start = (f32[1,9,1024]{2,1,0:T(8,128)S(1)}, f32[1,9,1024]{2,1,0:T(8,128)S(1)}, u32[]{:S(2)}, u32[]{:S(2)}) collective-permute-start(f32[1,9,1024]{2,1,0:T(8,128)S(1)} %maximum_bitcast_fusion.1), channel_id=1, source_target_pairs={{0,384},{32,416},{64,448},{96,480},{128,256},{160,288},{192,320},{... | collective-permute-start | bytes 110600 | tf_op jit(solution)/shard_map/ppermute | solution.py:26
  151.9 3.5 %collective-permute-start.1 = (f32[1,9,1024]{2,1,0:T(8,128)S(1)}, f32[1,9,1024]{2,1,0:T(8,128)S(1)}, u32[]{:S(2)}, u32[]{:S(2)}) collective-permute-start(f32[1,9,1024]{2,1,0:T(8,128)S(1)} %maximum_bitcast_fusion.1), channel_id=1, source_target_pairs={{0,256},{32,288},{64,320},{96,352},{128,384},{160,416},{192,448},{... | collective-permute-start | bytes 110600 | tf_op jit(solution)/shard_map/ppermute | solution.py:26
  155.4 2.7 collective-permute-start.2
  158.1 2.4 fusion.184
  160.5 2.4 collective-permute-done.1
  164.7 2.3 collective-permute-start.3
  167.0 4.4 %collective-permute-start.4 = (f32[2,2,1,9,1024]{4,3,1,0,2:T(8,128)S(1)}, f32[2,2,1,9,1024]{4,3,1,0,2:T(8,128)S(1)}, u32[]{:S(2)}, u32[]{:S(2)}) collective-permute-start(f32[2,2,1,9,1024]{4,3,1,0,2:T(8,128)S(1)} %bitcast.636), channel_id=1, source_target_pairs={{0,64},{32,96},{64,0},{96,32},{128,192},{160,224},{192,128},{224,1... | collective-permute-start | bytes 442376 | tf_op jit(solution)/shard_map/ppermute | solution.py:26
  171.5 2.5 collective-permute-start.5
  174.0 4.9 %fusion.4 = (f32[4,4,128]{2,1,0:T(4,128)S(1)}, f32[4,1024,128,4]{2,1,3,0:T(8,128)}) fusion(pred[128,1024]{0,1:T(8,128)(4,1)S(1)} %get-tuple-element.86, bf16[1024,4,128,1]{0,2,3,1:T(8,128)(2,1)S(1)} %bitcast.620, bf16[128,4,4,128]{3,2,1,0:T(4,128)(2,1)S(1)} %reshape_squeeze.3), kind=kOutput, calls=%fused_computation.12 | convolution fusion | flops 543160320 | bytes 10100736 | tf_op jit(solution)/shard_map/tgjd,ugd->gjtu/dot_general | solution.py:147
  178.8 2.3 collective-permute-done.4
  182.9 4.9 %collective-permute-start.6 = (bf16[1,8,1024]{2,1,0:T(8,128)(2,1)S(1)}, bf16[1,8,1024]{2,1,0:T(8,128)(2,1)S(1)}, u32[]{:S(2)}, u32[]{:S(2)}) collective-permute-start(bf16[1,8,1024]{2,1,0:T(8,128)(2,1)S(1)} %get-tuple-element.20), channel_id=1, source_target_pairs={{0,24},{1,25},{2,26},{3,27},{4,28},{5,29},{6,30},{7,31},{8,16},{9,... | collective-permute-start | bytes 49160 | tf_op jit(solution)/shard_map/ppermute | solution.py:26
  187.9 4.4 %collective-permute-start.7 = (bf16[1,8,1024]{2,1,0:T(8,128)(2,1)S(1)}, bf16[1,8,1024]{2,1,0:T(8,128)(2,1)S(1)}, u32[]{:S(2)}, u32[]{:S(2)}) collective-permute-start(bf16[1,8,1024]{2,1,0:T(8,128)(2,1)S(1)} %get-tuple-element.20), channel_id=1, source_target_pairs={{0,16},{1,17},{2,18},{3,19},{4,20},{5,21},{6,22},{7,23},{8,24},{9,... | collective-permute-start | bytes 49160 | tf_op jit(solution)/shard_map/ppermute | solution.py:26
  192.3 5.3 %collective-permute-start.8 = (bf16[1,8,1024]{2,1,0:T(8,128)(2,1)S(1)}, bf16[1,8,1024]{2,1,0:T(8,128)(2,1)S(1)}, u32[]{:S(2)}, u32[]{:S(2)}) collective-permute-start(bf16[1,8,1024]{2,1,0:T(8,128)(2,1)S(1)} %get-tuple-element.20), channel_id=1, source_target_pairs={{0,8},{1,9},{2,10},{3,11},{4,12},{5,13},{6,14},{7,15},{8,0},{9,1},... | collective-permute-start | bytes 49160 | tf_op jit(solution)/shard_map/ppermute | solution.py:26
  197.7 5.5 %fusion.3 = (f32[4,4,128]{2,1,0:T(4,128)}, f32[4,1024,128,4]{2,1,3,0:T(8,128)}) fusion(pred[128,1024]{0,1:T(8,128)(4,1)S(1)} %get-tuple-element.85, bf16[1024,4,128,1]{0,2,3,1:T(8,128)(2,1)S(1)} %bitcast.619, bf16[128,4,4,128]{3,2,1,0:T(4,128)(2,1)S(1)} %reshape_squeeze.3), kind=kOutput, calls=%fused_computation.11 | convolution fusion | flops 543160320 | bytes 10100736 | tf_op jit(solution)/shard_map/tgjd,ugd->gjtu/dot_general | solution.py:147
  203.2 4.0 %collective-permute-start.9 = (bf16[2,2,1,8,1024]{4,3,1,0,2:T(8,128)(2,1)S(1)}, bf16[2,2,1,8,1024]{4,3,1,0,2:T(8,128)(2,1)S(1)}, u32[]{:S(2)}, u32[]{:S(2)}) collective-permute-start(bf16[2,2,1,8,1024]{4,3,1,0,2:T(8,128)(2,1)S(1)} %bitcast.651), channel_id=1, source_target_pairs={{0,6},{1,7},{2,4},{3,5},{4,2},{5,3},{6,0},{7,1},{8,14},{9,15},{10,... | collective-permute-start | bytes 196616 | tf_op jit(solution)/shard_map/ppermute | solution.py:26
  207.3 2.7 collective-permute-start.10
  210.0 3.3 collective-permute-start.11
  213.3 5.5 %fusion.2 = (f32[4,4,128]{2,1,0:T(4,128)}, f32[4,1024,128,4]{2,1,3,0:T(8,128)}) fusion(pred[128,1024]{0,1:T(8,128)(4,1)S(1)} %get-tuple-element.87, bf16[1024,4,128,1]{0,2,3,1:T(8,128)(2,1)S(1)} %bitcast.618, bf16[128,4,4,128]{3,2,1,0:T(4,128)(2,1)S(1)} %reshape_squeeze.3), kind=kOutput, calls=%fused_computation.10 | convolution fusion | flops 543160320 | bytes 10100736 | tf_op jit(solution)/shard_map/tgjd,ugd->gjtu/dot_general | solution.py:147
  218.9 2.1 collective-permute-start.12
  221.1 4.8 %fusion.1 = (f32[4,4,128]{2,1,0:T(4,128)S(1)}, f32[4,1024,128,4]{2,1,3,0:T(8,128)}) fusion(pred[128,1024]{0,1:T(8,128)(4,1)S(1)} %copy-done.3, bf16[1024,4,128,1]{0,2,3,1:T(8,128)(2,1)S(1)} %bitcast.617, bf16[128,4,4,128]{3,2,1,0:T(4,128)(2,1)S(1)} %reshape_squeeze.3), kind=kOutput, calls=%fused_computation.9 | convolution fusion | flops 543160320 | bytes 10100736 | tf_op jit(solution)/shard_map/tgjd,ugd->gjtu/dot_general | solution.py:147
  230.2 4.6 %fusion.11 = f32[4,4,128]{2,1,0:T(4,128)S(1)} fusion(f32[4,1024,128,4]{2,1,3,0:T(8,128)} %get-tuple-element.94, f32[4,4,128]{2,1,0:T(4,128)S(1)} %get-tuple-element.17, pred[128,1024]{0,1:T(8,128)(4,1)S(1)} %get-tuple-element.86), kind=kLoop, calls=%fused_computation.19 | loop fusion | flops 10483712 | bytes 8536064 | tf_op jit(solution)/shard_map/reduce_sum | solution.py:70
  234.8 4.8 %fusion.9 = f32[4,4,128]{2,1,0:T(4,128)S(1)} fusion(f32[4,1024,128,4]{2,1,3,0:T(8,128)} %get-tuple-element.96, f32[4,4,128]{2,1,0:T(4,128)S(1)} %get-tuple-element.18, pred[128,1024]{0,1:T(8,128)(4,1)S(1)} %get-tuple-element.85), kind=kLoop, calls=%fused_computation.17 | loop fusion | flops 10483712 | bytes 8536064 | tf_op jit(solution)/shard_map/reduce_sum | solution.py:70
  242.0 2.0 fusion.5
  246.5 5.9 %fusion.64 = f32[128,4,4,128]{0,3,2,1:T(8,128)S(1)} fusion(bf16[1024,4,128,1]{0,2,3,1:T(8,128)(2,1)} %bitcast.634, f32[4,1024,128,4]{2,1,3,0:T(8,128)} %get-tuple-element.100, f32[4,4,128]{2,1,0:T(4,128)} %copy-done.52, pred[128,1024]{0,1:T(8,128)(4,1)} %get-tuple-element.88, f32[128,4,4]{0,2,1:T(4,128)} %get-tuple-element.80, ...), kind=kOutput, calls=%fused_computation.59 | convolution fusion | flops 547880960 | bytes 10641408 | tf_op jit(solution)/shard_map/gjtu,ugd->tgjd/dot_general | solution.py:153
  252.5 5.7 %fusion.67 = f32[128,4,4,128]{0,3,2,1:T(8,128)S(1)} fusion(f32[128,4,4,128]{0,3,2,1:T(8,128)S(1)} %fusion.64, bf16[1024,4,128,1]{0,2,3,1:T(8,128)(2,1)S(1)} %bitcast.633, f32[4,1024,128,4]{2,1,3,0:T(8,128)} %get-tuple-element.98, f32[4,4,128]{2,1,0:T(4,128)S(1)} %copy-done.21, pred[128,1024]{0,1:T(8,128)(4,1)S(1)} %get-tuple-element.87, ...), kind=kOutput, calls=%fused_computation.60 | convolution fusion | flops 547880960 | bytes 11681792 | tf_op jit(solution)/shard_map/gjtu,ugd->tgjd/dot_general | solution.py:153
  258.3 2.4 fusion.70
  260.8 2.6 fusion.73
  271.6 2.4 collective-permute-start.13
  275.6 4.0 %collective-permute-start.16 = (f32[4,8,1024]{2,1,0:T(8,128)S(1)}, f32[4,8,1024]{2,1,0:T(8,128)S(1)}, u32[]{:S(2)}, u32[]{:S(2)}) collective-permute-start(f32[4,8,1024]{2,1,0:T(8,128)S(1)} %get-tuple-element.56), channel_id=1, source_target_pairs={{0,6},{1,7},{2,4},{3,5},{4,2},{5,3},{6,0},{7,1},{8,14},{9,15},{10,... | collective-permute-start | bytes 393224 | tf_op jit(solution)/shard_map/ppermute | solution.py:53
  281.6 4.1 %collective-permute-start.14 = (f32[4,8,1024]{2,1,0:T(8,128)S(1)}, f32[4,8,1024]{2,1,0:T(8,128)S(1)}, u32[]{:S(2)}, u32[]{:S(2)}) collective-permute-start(f32[4,8,1024]{2,1,0:T(8,128)S(1)} %get-tuple-element.55), channel_id=1, source_target_pairs={{0,2},{1,3},{2,0},{3,1},{4,6},{5,7},{6,4},{7,5},{8,10},{9,11},{10,... | collective-permute-start | bytes 393224 | tf_op jit(solution)/shard_map/ppermute | solution.py:53
  285.8 6.1 %collective-permute-done.15 = f32[4,8,1024]{2,1,0:T(8,128)S(1)} collective-permute-done((f32[4,8,1024]{2,1,0:T(8,128)S(1)}, f32[4,8,1024]{2,1,0:T(8,128)S(1)}, u32[]{:S(2)}, u32[]{:S(2)}) %collective-permute-start.15) | collective-permute-done | bytes 131104 | tf_op jit(solution)/shard_map/ppermute | solution.py:53
  292.1 5.8 %collective-permute-start.19 = (f32[1,8,1024]{2,1,0:T(8,128)S(1)}, f32[1,8,1024]{2,1,0:T(8,128)S(1)}, u32[]{:S(2)}, u32[]{:S(2)}) collective-permute-start(f32[1,8,1024]{2,1,0:T(8,128)S(1)} %get-tuple-element.74), channel_id=1, source_target_pairs={{0,24},{1,25},{2,26},{3,27},{4,28},{5,29},{6,30},{7,31},{8,16},{9,... | collective-permute-start | bytes 98312 | tf_op jit(solution)/shard_map/ppermute | solution.py:53
  297.9 4.4 %collective-permute-start.18 = (f32[1,8,1024]{2,1,0:T(8,128)S(1)}, f32[1,8,1024]{2,1,0:T(8,128)S(1)}, u32[]{:S(2)}, u32[]{:S(2)}) collective-permute-start(f32[1,8,1024]{2,1,0:T(8,128)S(1)} %get-tuple-element.75), channel_id=1, source_target_pairs={{0,16},{1,17},{2,18},{3,19},{4,20},{5,21},{6,22},{7,23},{8,24},{9,... | collective-permute-start | bytes 98312 | tf_op jit(solution)/shard_map/ppermute | solution.py:53
  302.3 4.4 %collective-permute-start.17 = (f32[1,8,1024]{2,1,0:T(8,128)S(1)}, f32[1,8,1024]{2,1,0:T(8,128)S(1)}, u32[]{:S(2)}, u32[]{:S(2)}) collective-permute-start(f32[1,8,1024]{2,1,0:T(8,128)S(1)} %get-tuple-element.73), channel_id=1, source_target_pairs={{0,8},{1,9},{2,10},{3,11},{4,12},{5,13},{6,14},{7,15},{8,0},{9,1},... | collective-permute-start | bytes 98312 | tf_op jit(solution)/shard_map/ppermute | solution.py:53
  306.8 5.4 %collective-permute-done.17 = f32[1,8,1024]{2,1,0:T(8,128)S(1)} collective-permute-done((f32[1,8,1024]{2,1,0:T(8,128)S(1)}, f32[1,8,1024]{2,1,0:T(8,128)S(1)}, u32[]{:S(2)}, u32[]{:S(2)}) %collective-permute-start.17) | collective-permute-done | bytes 32800 | tf_op jit(solution)/shard_map/ppermute | solution.py:53
  312.2 3.3 collective-permute-start.20
  315.6 4.3 %collective-permute-start.21 = (f32[1,8,1024]{2,1,0:T(8,128)S(1)}, f32[1,8,1024]{2,1,0:T(8,128)S(1)}, u32[]{:S(2)}, u32[]{:S(2)}) collective-permute-start(f32[1,8,1024]{2,1,0:T(8,128)S(1)} %add_add_fusion), channel_id=1, source_target_pairs={{0,256},{32,288},{64,320},{96,352},{128,384},{160,416},{192,448},{... | collective-permute-start | bytes 98312 | tf_op jit(solution)/shard_map/ppermute | solution.py:26
  319.9 4.6 %collective-permute-start.22 = (f32[1,8,1024]{2,1,0:T(8,128)S(1)}, f32[1,8,1024]{2,1,0:T(8,128)S(1)}, u32[]{:S(2)}, u32[]{:S(2)}) collective-permute-start(f32[1,8,1024]{2,1,0:T(8,128)S(1)} %add_add_fusion), channel_id=1, source_target_pairs={{0,128},{32,160},{64,192},{96,224},{128,0},{160,32},{192,64},{224,... | collective-permute-start | bytes 98312 | tf_op jit(solution)/shard_map/ppermute | solution.py:26
  326.7 3.9 %collective-permute-start.23 = (f32[2,2,1,8,1024]{4,3,1,0,2:T(8,128)S(1)}, f32[2,2,1,8,1024]{4,3,1,0,2:T(8,128)S(1)}, u32[]{:S(2)}, u32[]{:S(2)}) collective-permute-start(f32[2,2,1,8,1024]{4,3,1,0,2:T(8,128)S(1)} %bitcast.645), channel_id=1, source_target_pairs={{0,96},{32,64},{64,32},{96,0},{128,224},{160,192},{192,160},{224,1... | collective-permute-start | bytes 393224 | tf_op jit(solution)/shard_map/ppermute | solution.py:26
  330.5 2.4 collective-permute-start.24
  332.9 3.0 collective-permute-start.25
  337.4 2.4 collective-permute-done.25
  (228 shorter events, 41.2 us)
Async XLA Ops:
  7.2 127.8 %copy-start = (bf16[8,512]{1,0:T(8,128)(2,1)S(1)}, bf16[8,512]{1,0:T(8,128)(2,1)}, u32[]{:S(2)}) copy-start(bf16[8,512]{1,0:T(8,128)(2,1)} %param.14) | copy-start | bytes 24580
  7.2 121.6 %all-gather.2.cloned.1.call-start = ((), (), s32[]{:S(2)}) async-start(), calls=%async_computation | async-start | bytes 8650752 | tf_op jit(solution)/shard_map/all_gather | solution.py:89
  138.0 20.0 %copy-start.2 = (bf16[4096,1024]{0,1:T(8,128)(2,1)S(1)}, bf16[4096,1024]{0,1:T(8,128)(2,1)}, u32[]{:S(2)}) copy-start(bf16[4096,1024]{0,1:T(8,128)(2,1)} %all-gather.2.cloned.1.call-done) | copy-start | bytes 25165828
  145.3 15.2 %collective-permute-start = (f32[1,9,1024]{2,1,0:T(8,128)S(1)}, f32[1,9,1024]{2,1,0:T(8,128)S(1)}, u32[]{:S(2)}, u32[]{:S(2)}) collective-permute-start(f32[1,9,1024]{2,1,0:T(8,128)S(1)} %maximum_bitcast_fusion.1), channel_id=1, source_target_pairs={{0,384},{32,416},{64,448},{96,480},{128,256},{160,288},{192,320},{... | collective-permute-start | bytes 110600 | tf_op jit(solution)/shard_map/ppermute | solution.py:26
  151.9 11.0 %collective-permute-start.1 = (f32[1,9,1024]{2,1,0:T(8,128)S(1)}, f32[1,9,1024]{2,1,0:T(8,128)S(1)}, u32[]{:S(2)}, u32[]{:S(2)}) collective-permute-start(f32[1,9,1024]{2,1,0:T(8,128)S(1)} %maximum_bitcast_fusion.1), channel_id=1, source_target_pairs={{0,256},{32,288},{64,320},{96,352},{128,384},{160,416},{192,448},{... | collective-permute-start | bytes 110600 | tf_op jit(solution)/shard_map/ppermute | solution.py:26
  155.4 9.2 %collective-permute-start.2 = (f32[1,9,1024]{2,1,0:T(8,128)S(1)}, f32[1,9,1024]{2,1,0:T(8,128)S(1)}, u32[]{:S(2)}, u32[]{:S(2)}) collective-permute-start(f32[1,9,1024]{2,1,0:T(8,128)S(1)} %maximum_bitcast_fusion.1), channel_id=1, source_target_pairs={{0,128},{32,160},{64,192},{96,224},{128,0},{160,32},{192,64},{224,... | collective-permute-start | bytes 110600 | tf_op jit(solution)/shard_map/ppermute | solution.py:26
  164.7 14.1 %collective-permute-start.3 = (f32[2,2,1,9,1024]{4,3,1,0,2:T(8,128)S(1)}, f32[2,2,1,9,1024]{4,3,1,0,2:T(8,128)S(1)}, u32[]{:S(2)}, u32[]{:S(2)}) collective-permute-start(f32[2,2,1,9,1024]{4,3,1,0,2:T(8,128)S(1)} %bitcast.635), channel_id=1, source_target_pairs={{0,96},{32,64},{64,32},{96,0},{128,224},{160,192},{192,160},{224,1... | collective-permute-start | bytes 442376 | tf_op jit(solution)/shard_map/ppermute | solution.py:26
  167.0 14.1 %collective-permute-start.4 = (f32[2,2,1,9,1024]{4,3,1,0,2:T(8,128)S(1)}, f32[2,2,1,9,1024]{4,3,1,0,2:T(8,128)S(1)}, u32[]{:S(2)}, u32[]{:S(2)}) collective-permute-start(f32[2,2,1,9,1024]{4,3,1,0,2:T(8,128)S(1)} %bitcast.636), channel_id=1, source_target_pairs={{0,64},{32,96},{64,0},{96,32},{128,192},{160,224},{192,128},{224,1... | collective-permute-start | bytes 442376 | tf_op jit(solution)/shard_map/ppermute | solution.py:26
  171.5 10.1 %collective-permute-start.5 = (f32[2,2,1,9,1024]{4,3,1,0,2:T(8,128)S(1)}, f32[2,2,1,9,1024]{4,3,1,0,2:T(8,128)S(1)}, u32[]{:S(2)}, u32[]{:S(2)}) collective-permute-start(f32[2,2,1,9,1024]{4,3,1,0,2:T(8,128)S(1)} %bitcast.637), channel_id=1, source_target_pairs={{0,32},{32,0},{64,96},{96,64},{128,160},{160,128},{192,224},{224,1... | collective-permute-start | bytes 442376 | tf_op jit(solution)/shard_map/ppermute | solution.py:26
  182.1 36.7 %copy-start.22 = (f32[1,1,1024]{2,1,0:T(1,128)}, f32[1,1,1024]{2,1,0:T(1,128)S(1)}, u32[]{:S(2)}) copy-start(f32[1,1,1024]{2,1,0:T(1,128)S(1)} %get-tuple-element.32) | copy-start | bytes 12292
  182.1 36.7 %copy-start.24 = (f32[1,1,1024]{2,1,0:T(1,128)}, f32[1,1,1024]{2,1,0:T(1,128)S(1)}, u32[]{:S(2)}) copy-start(f32[1,1,1024]{2,1,0:T(1,128)S(1)} %get-tuple-element.33) | copy-start | bytes 12292
  182.9 20.2 %collective-permute-start.6 = (bf16[1,8,1024]{2,1,0:T(8,128)(2,1)S(1)}, bf16[1,8,1024]{2,1,0:T(8,128)(2,1)S(1)}, u32[]{:S(2)}, u32[]{:S(2)}) collective-permute-start(bf16[1,8,1024]{2,1,0:T(8,128)(2,1)S(1)} %get-tuple-element.20), channel_id=1, source_target_pairs={{0,24},{1,25},{2,26},{3,27},{4,28},{5,29},{6,30},{7,31},{8,16},{9,... | collective-permute-start | bytes 49160 | tf_op jit(solution)/shard_map/ppermute | solution.py:26
  187.9 15.3 %collective-permute-start.7 = (bf16[1,8,1024]{2,1,0:T(8,128)(2,1)S(1)}, bf16[1,8,1024]{2,1,0:T(8,128)(2,1)S(1)}, u32[]{:S(2)}, u32[]{:S(2)}) collective-permute-start(bf16[1,8,1024]{2,1,0:T(8,128)(2,1)S(1)} %get-tuple-element.20), channel_id=1, source_target_pairs={{0,16},{1,17},{2,18},{3,19},{4,20},{5,21},{6,22},{7,23},{8,24},{9,... | collective-permute-start | bytes 49160 | tf_op jit(solution)/shard_map/ppermute | solution.py:26
  192.3 10.9 %collective-permute-start.8 = (bf16[1,8,1024]{2,1,0:T(8,128)(2,1)S(1)}, bf16[1,8,1024]{2,1,0:T(8,128)(2,1)S(1)}, u32[]{:S(2)}, u32[]{:S(2)}) collective-permute-start(bf16[1,8,1024]{2,1,0:T(8,128)(2,1)S(1)} %get-tuple-element.20), channel_id=1, source_target_pairs={{0,8},{1,9},{2,10},{3,11},{4,12},{5,13},{6,14},{7,15},{8,0},{9,1},... | collective-permute-start | bytes 49160 | tf_op jit(solution)/shard_map/ppermute | solution.py:26
  203.2 15.6 %collective-permute-start.9 = (bf16[2,2,1,8,1024]{4,3,1,0,2:T(8,128)(2,1)S(1)}, bf16[2,2,1,8,1024]{4,3,1,0,2:T(8,128)(2,1)S(1)}, u32[]{:S(2)}, u32[]{:S(2)}) collective-permute-start(bf16[2,2,1,8,1024]{4,3,1,0,2:T(8,128)(2,1)S(1)} %bitcast.651), channel_id=1, source_target_pairs={{0,6},{1,7},{2,4},{3,5},{4,2},{5,3},{6,0},{7,1},{8,14},{9,15},{10,... | collective-permute-start | bytes 196616 | tf_op jit(solution)/shard_map/ppermute | solution.py:26
  207.3 11.6 %collective-permute-start.10 = (bf16[2,2,1,8,1024]{4,3,1,0,2:T(8,128)(2,1)S(1)}, bf16[2,2,1,8,1024]{4,3,1,0,2:T(8,128)(2,1)S(1)}, u32[]{:S(2)}, u32[]{:S(2)}) collective-permute-start(bf16[2,2,1,8,1024]{4,3,1,0,2:T(8,128)(2,1)S(1)} %bitcast.652), channel_id=1, source_target_pairs={{0,4},{1,5},{2,6},{3,7},{4,0},{5,1},{6,2},{7,3},{8,12},{9,13},{10,... | collective-permute-start | bytes 196616 | tf_op jit(solution)/shard_map/ppermute | solution.py:26
  210.0 8.9 %collective-permute-start.11 = (bf16[2,2,1,8,1024]{4,3,1,0,2:T(8,128)(2,1)S(1)}, bf16[2,2,1,8,1024]{4,3,1,0,2:T(8,128)(2,1)S(1)}, u32[]{:S(2)}, u32[]{:S(2)}) collective-permute-start(bf16[2,2,1,8,1024]{4,3,1,0,2:T(8,128)(2,1)S(1)} %bitcast.653), channel_id=1, source_target_pairs={{0,2},{1,3},{2,0},{3,1},{4,6},{5,7},{6,4},{7,5},{8,10},{9,11},{10,... | collective-permute-start | bytes 196616 | tf_op jit(solution)/shard_map/ppermute | solution.py:26
  218.9 6.9 %collective-permute-start.12 = (bf16[2,2,2,2,1,8,1024]{6,5,3,2,1,0,4:T(8,128)(2,1)S(1)}, bf16[2,2,2,2,1,8,1024]{6,5,3,2,1,0,4:T(8,128)(2,1)S(1)}, u32[]{:S(2)}, u32[]{:S(2)}) collective-permute-start(bf16[2,2,2,2,1,8,1024]{6,5,3,2,1,0,4:T(8,128)(2,1)S(1)} %bitcast.639), channel_id=1, source_target_pairs={{0,1},{1,0},{2,3},{3,2},{4,5},{5,4},{6,7},{7,6},{8,9},{9,8},{10,11... | collective-permute-start | bytes 786440 | tf_op jit(solution)/shard_map/ppermute | solution.py:26
  266.3 74.5 %copy-start.1 = (bf16[8,512]{1,0:T(8,128)(2,1)S(1)}, bf16[8,512]{1,0:T(8,128)(2,1)}, u32[]{:S(2)}) copy-start(bf16[8,512]{1,0:T(8,128)(2,1)} %param.14) | copy-start | bytes 24580
  268.1 67.8 %copy-start.8 = (bf16[128,4,4,128]{0,3,2,1:T(8,128)(2,1)S(1)}, bf16[128,4,4,128]{0,3,2,1:T(8,128)(2,1)}, u32[]{:S(2)}) copy-start(bf16[128,4,4,128]{0,3,2,1:T(8,128)(2,1)} %get-tuple-element.101) | copy-start | bytes 1572868
  268.1 71.9 %copy-start.23 = (f32[1,1,1024]{2,1,0:T(1,128)S(1)}, f32[1,1,1024]{2,1,0:T(1,128)}, u32[]{:S(2)}) copy-start(f32[1,1,1024]{2,1,0:T(1,128)} %copy-done.22) | copy-start | bytes 12292
  268.1 71.9 %copy-start.25 = (f32[1,1,1024]{2,1,0:T(1,128)S(1)}, f32[1,1,1024]{2,1,0:T(1,128)}, u32[]{:S(2)}) copy-start(f32[1,1,1024]{2,1,0:T(1,128)} %copy-done.24) | copy-start | bytes 12292
  268.1 71.9 %copy-start.27 = (f32[1,1,1024]{2,1,0:T(1,128)S(1)}, f32[1,1,1024]{2,1,0:T(1,128)}, u32[]{:S(2)}) copy-start(f32[1,1,1024]{2,1,0:T(1,128)} %copy-done.26) | copy-start | bytes 12292
  268.1 71.9 %copy-start.29 = (f32[1,1,1024]{2,1,0:T(1,128)S(1)}, f32[1,1,1024]{2,1,0:T(1,128)}, u32[]{:S(2)}) copy-start(f32[1,1,1024]{2,1,0:T(1,128)} %copy-done.28) | copy-start | bytes 12292
  268.1 71.9 %copy-start.31 = (f32[1,1,1024]{2,1,0:T(1,128)S(1)}, f32[1,1,1024]{2,1,0:T(1,128)}, u32[]{:S(2)}) copy-start(f32[1,1,1024]{2,1,0:T(1,128)} %copy-done.30) | copy-start | bytes 12292
  268.2 71.9 %copy-start.33 = (f32[1,1,1024]{2,1,0:T(1,128)S(1)}, f32[1,1,1024]{2,1,0:T(1,128)}, u32[]{:S(2)}) copy-start(f32[1,1,1024]{2,1,0:T(1,128)} %copy-done.32) | copy-start | bytes 12292
  268.2 71.9 %copy-start.35 = (f32[1,1,1024]{2,1,0:T(1,128)S(1)}, f32[1,1,1024]{2,1,0:T(1,128)}, u32[]{:S(2)}) copy-start(f32[1,1,1024]{2,1,0:T(1,128)} %copy-done.34) | copy-start | bytes 12292
  268.2 71.9 %copy-start.37 = (f32[1,1,1024]{2,1,0:T(1,128)S(1)}, f32[1,1,1024]{2,1,0:T(1,128)}, u32[]{:S(2)}) copy-start(f32[1,1,1024]{2,1,0:T(1,128)} %copy-done.36) | copy-start | bytes 12292
  268.2 71.9 %copy-start.39 = (f32[1,1,1024]{2,1,0:T(1,128)S(1)}, f32[1,1,1024]{2,1,0:T(1,128)}, u32[]{:S(2)}) copy-start(f32[1,1,1024]{2,1,0:T(1,128)} %copy-done.38) | copy-start | bytes 12292
  268.2 71.9 %copy-start.41 = (f32[1,1,1024]{2,1,0:T(1,128)S(1)}, f32[1,1,1024]{2,1,0:T(1,128)}, u32[]{:S(2)}) copy-start(f32[1,1,1024]{2,1,0:T(1,128)} %copy-done.40) | copy-start | bytes 12292
  268.2 71.9 %copy-start.43 = (f32[1,1,1024]{2,1,0:T(1,128)S(1)}, f32[1,1,1024]{2,1,0:T(1,128)}, u32[]{:S(2)}) copy-start(f32[1,1,1024]{2,1,0:T(1,128)} %copy-done.42) | copy-start | bytes 12292
  268.2 71.9 %copy-start.45 = (f32[1,1,1024]{2,1,0:T(1,128)S(1)}, f32[1,1,1024]{2,1,0:T(1,128)}, u32[]{:S(2)}) copy-start(f32[1,1,1024]{2,1,0:T(1,128)} %copy-done.44) | copy-start | bytes 12292
  268.2 71.9 %copy-start.47 = (f32[1,1,1024]{2,1,0:T(1,128)S(1)}, f32[1,1,1024]{2,1,0:T(1,128)}, u32[]{:S(2)}) copy-start(f32[1,1,1024]{2,1,0:T(1,128)} %copy-done.46) | copy-start | bytes 12292
  268.2 71.9 %copy-start.49 = (f32[1,1,1024]{2,1,0:T(1,128)S(1)}, f32[1,1,1024]{2,1,0:T(1,128)}, u32[]{:S(2)}) copy-start(f32[1,1,1024]{2,1,0:T(1,128)} %copy-done.48) | copy-start | bytes 12292
  268.2 71.9 %copy-start.51 = (f32[1,1,1024]{2,1,0:T(1,128)S(1)}, f32[1,1,1024]{2,1,0:T(1,128)}, u32[]{:S(2)}) copy-start(f32[1,1,1024]{2,1,0:T(1,128)} %copy-done.50) | copy-start | bytes 12292
  271.6 3.9 %collective-permute-start.13 = (f32[16,8,1024]{2,1,0:T(8,128)S(1)}, f32[16,8,1024]{2,1,0:T(8,128)S(1)}, u32[]{:S(2)}, u32[]{:S(2)}) collective-permute-start(f32[16,8,1024]{2,1,0:T(8,128)S(1)} %dynamic-slice_bitcast_fusion), channel_id=1, source_target_pairs={{0,1},{1,0},{2,3},{3,2},{4,5},{5,4},{6,7},{7,6},{8,9},{9,8},{10,11... | collective-permute-start | bytes 1572872 | tf_op jit(solution)/shard_map/ppermute | solution.py:53
  275.6 10.2 %collective-permute-start.16 = (f32[4,8,1024]{2,1,0:T(8,128)S(1)}, f32[4,8,1024]{2,1,0:T(8,128)S(1)}, u32[]{:S(2)}, u32[]{:S(2)}) collective-permute-start(f32[4,8,1024]{2,1,0:T(8,128)S(1)} %get-tuple-element.56), channel_id=1, source_target_pairs={{0,6},{1,7},{2,4},{3,5},{4,2},{5,3},{6,0},{7,1},{8,14},{9,15},{10,... | collective-permute-start | bytes 393224 | tf_op jit(solution)/shard_map/ppermute | solution.py:53
  279.7 12.2 %collective-permute-start.15 = (f32[4,8,1024]{2,1,0:T(8,128)S(1)}, f32[4,8,1024]{2,1,0:T(8,128)S(1)}, u32[]{:S(2)}, u32[]{:S(2)}) collective-permute-start(f32[4,8,1024]{2,1,0:T(8,128)S(1)} %get-tuple-element.57), channel_id=1, source_target_pairs={{0,4},{1,5},{2,6},{3,7},{4,0},{5,1},{6,2},{7,3},{8,12},{9,13},{10,... | collective-permute-start | bytes 393224 | tf_op jit(solution)/shard_map/ppermute | solution.py:53
  281.6 10.4 %collective-permute-start.14 = (f32[4,8,1024]{2,1,0:T(8,128)S(1)}, f32[4,8,1024]{2,1,0:T(8,128)S(1)}, u32[]{:S(2)}, u32[]{:S(2)}) collective-permute-start(f32[4,8,1024]{2,1,0:T(8,128)S(1)} %get-tuple-element.55), channel_id=1, source_target_pairs={{0,2},{1,3},{2,0},{3,1},{4,6},{5,7},{6,4},{7,5},{8,10},{9,11},{10,... | collective-permute-start | bytes 393224 | tf_op jit(solution)/shard_map/ppermute | solution.py:53
  292.1 14.7 %collective-permute-start.19 = (f32[1,8,1024]{2,1,0:T(8,128)S(1)}, f32[1,8,1024]{2,1,0:T(8,128)S(1)}, u32[]{:S(2)}, u32[]{:S(2)}) collective-permute-start(f32[1,8,1024]{2,1,0:T(8,128)S(1)} %get-tuple-element.74), channel_id=1, source_target_pairs={{0,24},{1,25},{2,26},{3,27},{4,28},{5,29},{6,30},{7,31},{8,16},{9,... | collective-permute-start | bytes 98312 | tf_op jit(solution)/shard_map/ppermute | solution.py:53
  297.9 8.8 %collective-permute-start.18 = (f32[1,8,1024]{2,1,0:T(8,128)S(1)}, f32[1,8,1024]{2,1,0:T(8,128)S(1)}, u32[]{:S(2)}, u32[]{:S(2)}) collective-permute-start(f32[1,8,1024]{2,1,0:T(8,128)S(1)} %get-tuple-element.75), channel_id=1, source_target_pairs={{0,16},{1,17},{2,18},{3,19},{4,20},{5,21},{6,22},{7,23},{8,24},{9,... | collective-permute-start | bytes 98312 | tf_op jit(solution)/shard_map/ppermute | solution.py:53
  302.3 9.9 %collective-permute-start.17 = (f32[1,8,1024]{2,1,0:T(8,128)S(1)}, f32[1,8,1024]{2,1,0:T(8,128)S(1)}, u32[]{:S(2)}, u32[]{:S(2)}) collective-permute-start(f32[1,8,1024]{2,1,0:T(8,128)S(1)} %get-tuple-element.73), channel_id=1, source_target_pairs={{0,8},{1,9},{2,10},{3,11},{4,12},{5,13},{6,14},{7,15},{8,0},{9,1},... | collective-permute-start | bytes 98312 | tf_op jit(solution)/shard_map/ppermute | solution.py:53
  312.2 12.2 %collective-permute-start.20 = (f32[1,8,1024]{2,1,0:T(8,128)S(1)}, f32[1,8,1024]{2,1,0:T(8,128)S(1)}, u32[]{:S(2)}, u32[]{:S(2)}) collective-permute-start(f32[1,8,1024]{2,1,0:T(8,128)S(1)} %add_add_fusion), channel_id=1, source_target_pairs={{0,384},{32,416},{64,448},{96,480},{128,256},{160,288},{192,320},{... | collective-permute-start | bytes 98312 | tf_op jit(solution)/shard_map/ppermute | solution.py:26
  315.6 10.0 %collective-permute-start.21 = (f32[1,8,1024]{2,1,0:T(8,128)S(1)}, f32[1,8,1024]{2,1,0:T(8,128)S(1)}, u32[]{:S(2)}, u32[]{:S(2)}) collective-permute-start(f32[1,8,1024]{2,1,0:T(8,128)S(1)} %add_add_fusion), channel_id=1, source_target_pairs={{0,256},{32,288},{64,320},{96,352},{128,384},{160,416},{192,448},{... | collective-permute-start | bytes 98312 | tf_op jit(solution)/shard_map/ppermute | solution.py:26
  319.9 6.7 %collective-permute-start.22 = (f32[1,8,1024]{2,1,0:T(8,128)S(1)}, f32[1,8,1024]{2,1,0:T(8,128)S(1)}, u32[]{:S(2)}, u32[]{:S(2)}) collective-permute-start(f32[1,8,1024]{2,1,0:T(8,128)S(1)} %add_add_fusion), channel_id=1, source_target_pairs={{0,128},{32,160},{64,192},{96,224},{128,0},{160,32},{192,64},{224,... | collective-permute-start | bytes 98312 | tf_op jit(solution)/shard_map/ppermute | solution.py:26
  326.7 10.3 %collective-permute-start.23 = (f32[2,2,1,8,1024]{4,3,1,0,2:T(8,128)S(1)}, f32[2,2,1,8,1024]{4,3,1,0,2:T(8,128)S(1)}, u32[]{:S(2)}, u32[]{:S(2)}) collective-permute-start(f32[2,2,1,8,1024]{4,3,1,0,2:T(8,128)S(1)} %bitcast.645), channel_id=1, source_target_pairs={{0,96},{32,64},{64,32},{96,0},{128,224},{160,192},{192,160},{224,1... | collective-permute-start | bytes 393224 | tf_op jit(solution)/shard_map/ppermute | solution.py:26
  330.5 6.9 %collective-permute-start.24 = (f32[2,2,1,8,1024]{4,3,1,0,2:T(8,128)S(1)}, f32[2,2,1,8,1024]{4,3,1,0,2:T(8,128)S(1)}, u32[]{:S(2)}, u32[]{:S(2)}) collective-permute-start(f32[2,2,1,8,1024]{4,3,1,0,2:T(8,128)S(1)} %bitcast.646), channel_id=1, source_target_pairs={{0,64},{32,96},{64,0},{96,32},{128,192},{160,224},{192,128},{224,1... | collective-permute-start | bytes 393224 | tf_op jit(solution)/shard_map/ppermute | solution.py:26
  332.9 6.9 %collective-permute-start.25 = (f32[2,2,1,8,1024]{4,3,1,0,2:T(8,128)S(1)}, f32[2,2,1,8,1024]{4,3,1,0,2:T(8,128)S(1)}, u32[]{:S(2)}, u32[]{:S(2)}) collective-permute-start(f32[2,2,1,8,1024]{4,3,1,0,2:T(8,128)S(1)} %bitcast.647), channel_id=1, source_target_pairs={{0,32},{32,0},{64,96},{96,64},{128,160},{160,128},{192,224},{224,1... | collective-permute-start | bytes 393224 | tf_op jit(solution)/shard_map/ppermute | solution.py:26
  (46 other events, 444.2 us)
Sparse Core Ops, SparseCore 0:
  11.7 117.0 all-gather.1
where the time goes:
time: 349 us; the launch traced here: 348 us
  waiting for transfers between devices  132 us (38%)
  starting transfers between devices  97.4 us (28%)
  matrix products  53.2 us (15%)
  other arithmetic  24.5 us (7%)
  local copies, waits for them, and re-layouts  24.4 us (7%)
  between operations  16.4 us (5%)
    all_gather x1, waiting for transfers between devices, shards(): lax.all_gather(jnp.concatenate([seg_keys[0], seg_values[0]], axis=1), 'to...  107 us
    ppermute x19, starting transfers between devices, gathered(): lax.ppermute(held, axis, [(i, i ^ flip) for i in range(size)])  70.2 us
    ppermute x7, starting transfers between devices, scattered_sum(): lax.ppermute(send, axis, [(i, i ^ flip) for i in range(size)])  27.1 us
    dot_general x4, matrix products, shards(): jnp.einsum('tgjd,ugd->gjtu', queries, key_block, preferred_element_type=j...  20.6 us
    dot_general x4, matrix products, shards(): jnp.einsum('gjtu,ugd->tgjd', seg_weights, value_block, preferred_element_...  16.5 us
    reduce_sum x4, other arithmetic, softmax_step(): new_total = row_total * multiplier + jnp.sum(weights, axis=-1)  13.4 us
    ppermute x7, waiting for transfers between devices, scattered_sum(): lax.ppermute(send, axis, [(i, i ^ flip) for i in range(size)])  13.2 us
    ppermute x19, waiting for transfers between devices, gathered(): lax.ppermute(held, axis, [(i, i ^ flip) for i in range(size)])  11.8 us
  transfers between devices with their start and end apart: 27, of which 13 were waited for; matrix products, arithmetic and copies ran while one was open for 10% of the time, Pallas kernels for 0%

commit v1 on v0

--- a/solution.py
+++ b/solution.py
@@ -86,9 +86,16 @@
     queries = seg_queries[0].reshape(tok_rows, KVH, group_size, HD)
     slot_queries = mem_query.reshape(mem_rows, KVH, HD)
     row_pos = tok_index * tok_rows + jnp.arange(tok_rows)
-    kv_piece = lax.all_gather(
-        jnp.concatenate([seg_keys[0], seg_values[0]], axis=1), "tok", axis=0, tiled=True
-    )
+    advance_rows = lambda chunk, ax_name, dimension_no: jnp.concatenate(
+        lax.all_to_all(
+            jnp.stack([chunk for _ in range(lax.psum(1, ax_name))]),
+            ax_name,
+            split_axis=0,
+            concat_axis=0,
+        ),
+        dimension_no,
+    )
+    kv_piece = advance_rows(jnp.concatenate([seg_keys[0], seg_values[0]], axis=1), "tok", 0)
     piece_rows = kv_piece.shape[0]
     key_piece = kv_piece[:, :width_kv].reshape(piece_rows, KVH, HD)
     value_piece = kv_piece[:, width_kv:].reshape(piece_rows, KVH, HD)

time: 349 us -> 429 us (1.23)
  the two profiles are of different devices: /device:TPU:2 before, /device:TPU:4 now
where the time goes in v1:
time: 429 us; the launch traced here: 428 us
  waiting for transfers between devices  199 us (46%)
  starting transfers between devices  117 us (27%)
  matrix products  53.2 us (12%)
  local copies, waits for them, and re-layouts  32.3 us (8%)
  other arithmetic  24.2 us (6%)
    all_to_all x1, waiting for transfers between devices, shards(): lax.all_to_all(jnp.stack([chunk for _ in range(lax.psum(1, ax_name))]), a...  177 us
    ppermute x19, starting transfers between devices, gathered(): lax.ppermute(held, axis, [(i, i ^ flip) for i in range(size)])  78.7 us
    ppermute x7, starting transfers between devices, scattered_sum(): lax.ppermute(send, axis, [(i, i ^ flip) for i in range(size)])  27.1 us
    dot_general x4, matrix products, shards(): jnp.einsum('tgjd,ugd->gjtu', queries, key_block, preferred_element_type=j...  20.6 us
    dot_general x4, matrix products, shards(): jnp.einsum('gjtu,ugd->tgjd', seg_weights, value_block, preferred_element_...  16.6 us
    reduce_sum x4, other arithmetic, softmax_step(): new_total = row_total * multiplier + jnp.sum(weights, axis=-1)  13.4 us
    ppermute x7, waiting for transfers between devices, scattered_sum(): lax.ppermute(send, axis, [(i, i ^ flip) for i in range(size)])  13 us
    all_to_all x1, starting transfers between devices, shards(): lax.all_to_all(jnp.stack([chunk for _ in range(lax.psum(1, ax_name))]), a...  10.6 us
  transfers between devices with their start and end apart: 27, of which 11 were waited for; matrix products, arithmetic and copies ran while one was open for 7% of the time, Pallas kernels for 0%

profile of v1, /device:TPU:4, one launch (start us, length us, event | category | flops | bytes accessed | tf_op | source)
XLA Modules:
  0.0 427.8 jit_solution(13071201661787621116)
XLA Ops:
  1.8 5.2 %stack.134 = bf16[32,128,1024]{1,2,0:T(8,128)(2,1)} broadcast(bf16[128,1024]{0,1:T(8,128)(2,1)S(1)} %copy.106), dimensions={1,2} | broadcast | bytes 8650752 | tf_op jit(solution)/shard_map/stack | solution.py:91
  7.1 10.6 %all-to-all-start = ((bf16[32,128,1024]{1,2,0:T(8,128)(2,1)}), bf16[32,128,1024]{1,2,0:T(8,128)(2,1)}, u32[]{:S(2)}, u32[]{:S(2)}) async-start(bf16[32,128,1024]{1,2,0:T(8,128)(2,1)} %stack.134), calls=%async_computation | async-start | bytes 16777216 | tf_op jit(solution)/shard_map/all_to_all | solution.py:90
  23.6 2.2 compare_and_fusion.1
  25.8 176.7 %all-to-all-done = bf16[32,128,1024]{1,2,0:T(8,128)(2,1)} async-done(((bf16[32,128,1024]{1,2,0:T(8,128)(2,1)}), bf16[32,128,1024]{1,2,0:T(8,128)(2,1)}, u32[]{:S(2)}, u32[]{:S(2)}) %all-to-all-start) | async-done | bytes 8388640 | tf_op jit(solution)/shard_map/all_to_all | solution.py:90
  202.5 8.0 %copy_bitcast_fusion = bf16[4096,1024]{0,1:T(8,128)(2,1)} fusion(bf16[32,128,1024]{1,2,0:T(8,128)(2,1)} %all-to-all-done), kind=kLoop, calls=%fused_computation.1 | loop fusion | bytes 16777216 | tf_op jit(solution)/shard_map/reshape | solution.py:89
  210.5 6.1 %fusion.185 = (bf16[4096,512]{0,1:T(8,128)(2,1)}, bf16[4096,512]{0,1:T(8,128)(2,1)}) fusion(bf16[4096,1024]{0,1:T(8,128)(2,1)} %copy_bitcast_fusion), kind=kLoop, calls=%fused_computation.283 | loop fusion | bytes 16777216 | tf_op jit(solution)/shard_map/slice | solution.py:100
  216.6 3.1 fusion.188
  219.7 3.5 fusion.80
  223.2 3.5 fusion.79
  226.9 10.7 %collective-permute-start = (f32[1,9,1024]{2,1,0:T(8,128)S(1)}, f32[1,9,1024]{2,1,0:T(8,128)S(1)}, u32[]{:S(2)}, u32[]{:S(2)}) collective-permute-start(f32[1,9,1024]{2,1,0:T(8,128)S(1)} %maximum_bitcast_fusion.1), channel_id=1, source_target_pairs={{0,384},{32,416},{64,448},{96,480},{128,256},{160,288},{192,320},{... | collective-permute-start | bytes 110600 | tf_op jit(solution)/shard_map/ppermute | solution.py:26
  237.6 1.9 collective-permute-start.1
  239.6 4.3 collective-permute-start.2
  243.9 2.4 fusion.184
  246.3 2.1 collective-permute-done.1
  248.5 4.1 collective-permute-start.3
  252.6 2.3 collective-permute-start.4
  255.0 2.7 collective-permute-start.5
  257.7 4.9 %fusion.4 = (f32[4,4,128]{2,1,0:T(4,128)S(1)}, f32[4,1024,128,4]{2,1,3,0:T(8,128)}) fusion(pred[128,1024]{0,1:T(8,128)(4,1)S(1)} %get-tuple-element.89, bf16[1024,4,128,1]{0,2,3,1:T(8,128)(2,1)S(1)} %bitcast.625, bf16[128,4,4,128]{3,2,1,0:T(4,128)(2,1)S(1)} %reshape_squeeze.3), kind=kOutput, calls=%fused_computation.13 | convolution fusion | flops 543160320 | bytes 10100736 | tf_op jit(solution)/shard_map/tgjd,ugd->gjtu/dot_general | solution.py:154
  265.3 5.0 %collective-permute-start.6 = (bf16[1,8,1024]{2,1,0:T(8,128)(2,1)S(1)}, bf16[1,8,1024]{2,1,0:T(8,128)(2,1)S(1)}, u32[]{:S(2)}, u32[]{:S(2)}) collective-permute-start(bf16[1,8,1024]{2,1,0:T(8,128)(2,1)S(1)} %get-tuple-element.23), channel_id=1, source_target_pairs={{0,24},{1,25},{2,26},{3,27},{4,28},{5,29},{6,30},{7,31},{8,16},{9,... | collective-permute-start | bytes 49160 | tf_op jit(solution)/shard_map/ppermute | solution.py:26
  270.3 5.2 %collective-permute-start.7 = (bf16[1,8,1024]{2,1,0:T(8,128)(2,1)S(1)}, bf16[1,8,1024]{2,1,0:T(8,128)(2,1)S(1)}, u32[]{:S(2)}, u32[]{:S(2)}) collective-permute-start(bf16[1,8,1024]{2,1,0:T(8,128)(2,1)S(1)} %get-tuple-element.23), channel_id=1, source_target_pairs={{0,16},{1,17},{2,18},{3,19},{4,20},{5,21},{6,22},{7,23},{8,24},{9,... | collective-permute-start | bytes 49160 | tf_op jit(solution)/shard_map/ppermute | solution.py:26
  275.5 4.6 %collective-permute-start.8 = (bf16[1,8,1024]{2,1,0:T(8,128)(2,1)S(1)}, bf16[1,8,1024]{2,1,0:T(8,128)(2,1)S(1)}, u32[]{:S(2)}, u32[]{:S(2)}) collective-permute-start(bf16[1,8,1024]{2,1,0:T(8,128)(2,1)S(1)} %get-tuple-element.23), channel_id=1, source_target_pairs={{0,8},{1,9},{2,10},{3,11},{4,12},{5,13},{6,14},{7,15},{8,0},{9,1},... | collective-permute-start | bytes 49160 | tf_op jit(solution)/shard_map/ppermute | solution.py:26
  280.2 5.4 %fusion.3 = (f32[4,4,128]{2,1,0:T(4,128)}, f32[4,1024,128,4]{2,1,3,0:T(8,128)}) fusion(pred[128,1024]{0,1:T(8,128)(4,1)S(1)} %get-tuple-element.88, bf16[1024,4,128,1]{0,2,3,1:T(8,128)(2,1)S(1)} %bitcast.624, bf16[128,4,4,128]{3,2,1,0:T(4,128)(2,1)S(1)} %reshape_squeeze.3), kind=kOutput, calls=%fused_computation.12 | convolution fusion | flops 543160320 | bytes 10100736 | tf_op jit(solution)/shard_map/tgjd,ugd->gjtu/dot_general | solution.py:154
  285.8 10.0 %collective-permute-start.9 = (bf16[2,2,1,8,1024]{4,3,1,0,2:T(8,128)(2,1)S(1)}, bf16[2,2,1,8,1024]{4,3,1,0,2:T(8,128)(2,1)S(1)}, u32[]{:S(2)}, u32[]{:S(2)}) collective-permute-start(bf16[2,2,1,8,1024]{4,3,1,0,2:T(8,128)(2,1)S(1)} %bitcast.654), channel_id=1, source_target_pairs={{0,6},{1,7},{2,4},{3,5},{4,2},{5,3},{6,0},{7,1},{8,14},{9,15},{10,... | collective-permute-start | bytes 196616 | tf_op jit(solution)/shard_map/ppermute | solution.py:26
  297.7 2.5 collective-permute-start.11
  300.1 5.5 %fusion.2 = (f32[4,4,128]{2,1,0:T(4,128)}, f32[4,1024,128,4]{2,1,3,0:T(8,128)}) fusion(pred[128,1024]{0,1:T(8,128)(4,1)S(1)} %get-tuple-element.90, bf16[1024,4,128,1]{0,2,3,1:T(8,128)(2,1)S(1)} %bitcast.623, bf16[128,4,4,128]{3,2,1,0:T(4,128)(2,1)S(1)} %reshape_squeeze.3), kind=kOutput, calls=%fused_computation.11 | convolution fusion | flops 543160320 | bytes 10100736 | tf_op jit(solution)/shard_map/tgjd,ugd->gjtu/dot_general | solution.py:154
  307.7 4.8 %fusion.1 = (f32[4,4,128]{2,1,0:T(4,128)S(1)}, f32[4,1024,128,4]{2,1,3,0:T(8,128)}) fusion(pred[128,1024]{0,1:T(8,128)(4,1)S(1)} %copy-done.3, bf16[1024,4,128,1]{0,2,3,1:T(8,128)(2,1)S(1)} %bitcast.622, bf16[128,4,4,128]{3,2,1,0:T(4,128)(2,1)S(1)} %reshape_squeeze.3), kind=kOutput, calls=%fused_computation.10 | convolution fusion | flops 543160320 | bytes 10100736 | tf_op jit(solution)/shard_map/tgjd,ugd->gjtu/dot_general | solution.py:154
  316.7 4.8 %fusion.11 = f32[4,4,128]{2,1,0:T(4,128)S(1)} fusion(f32[4,1024,128,4]{2,1,3,0:T(8,128)} %get-tuple-element.97, f32[4,4,128]{2,1,0:T(4,128)S(1)} %get-tuple-element.20, pred[128,1024]{0,1:T(8,128)(4,1)S(1)} %get-tuple-element.89), kind=kLoop, calls=%fused_computation.20 | loop fusion | flops 10483712 | bytes 8536064 | tf_op jit(solution)/shard_map/reduce_sum | solution.py:70
  321.6 4.6 %fusion.9 = f32[4,4,128]{2,1,0:T(4,128)S(1)} fusion(f32[4,1024,128,4]{2,1,3,0:T(8,128)} %get-tuple-element.99, f32[4,4,128]{2,1,0:T(4,128)S(1)} %get-tuple-element.21, pred[128,1024]{0,1:T(8,128)(4,1)S(1)} %get-tuple-element.88), kind=kLoop, calls=%fused_computation.18 | loop fusion | flops 10483712 | bytes 8536064 | tf_op jit(solution)/shard_map/reduce_sum | solution.py:70
  326.5 2.0 fusion.7
  328.6 2.0 fusion.5
  333.1 5.9 %fusion.64 = f32[128,4,4,128]{0,3,2,1:T(8,128)S(1)} fusion(bf16[1024,4,128,1]{0,2,3,1:T(8,128)(2,1)} %bitcast.639, f32[4,1024,128,4]{2,1,3,0:T(8,128)} %get-tuple-element.103, f32[4,4,128]{2,1,0:T(4,128)} %copy-done.54, pred[128,1024]{0,1:T(8,128)(4,1)} %get-tuple-element.91, f32[128,4,4]{0,2,1:T(4,128)} %get-tuple-element.83, ...), kind=kOutput, calls=%fused_computation.60 | convolution fusion | flops 547880960 | bytes 10641408 | tf_op jit(solution)/shard_map/gjtu,ugd->tgjd/dot_general | solution.py:160
  339.1 5.7 %fusion.67 = f32[128,4,4,128]{0,3,2,1:T(8,128)S(1)} fusion(f32[128,4,4,128]{0,3,2,1:T(8,128)S(1)} %fusion.64, bf16[1024,4,128,1]{0,2,3,1:T(8,128)(2,1)S(1)} %bitcast.638, f32[4,1024,128,4]{2,1,3,0:T(8,128)} %get-tuple-element.101, f32[4,4,128]{2,1,0:T(4,128)S(1)} %copy-done.23, pred[128,1024]{0,1:T(8,128)(4,1)S(1)} %get-tuple-element.90, ...), kind=kOutput, calls=%fused_computation.61 | convolution fusion | flops 547880960 | bytes 11681792 | tf_op jit(solution)/shard_map/gjtu,ugd->tgjd/dot_general | solution.py:160
  344.9 2.4 fusion.70
  347.4 2.6 fusion.73
  358.2 2.4 collective-permute-start.13
  362.2 5.7 %collective-permute-start.16 = (f32[4,8,1024]{2,1,0:T(8,128)S(1)}, f32[4,8,1024]{2,1,0:T(8,128)S(1)}, u32[]{:S(2)}, u32[]{:S(2)}) collective-permute-start(f32[4,8,1024]{2,1,0:T(8,128)S(1)} %get-tuple-element.59), channel_id=1, source_target_pairs={{0,6},{1,7},{2,4},{3,5},{4,2},{5,3},{6,0},{7,1},{8,14},{9,15},{10,... | collective-permute-start | bytes 393224 | tf_op jit(solution)/shard_map/ppermute | solution.py:53
  369.9 2.5 collective-permute-start.14
  372.4 6.9 %collective-permute-done.15 = f32[4,8,1024]{2,1,0:T(8,128)S(1)} collective-permute-done((f32[4,8,1024]{2,1,0:T(8,128)S(1)}, f32[4,8,1024]{2,1,0:T(8,128)S(1)}, u32[]{:S(2)}, u32[]{:S(2)}) %collective-permute-start.15) | collective-permute-done | bytes 131104 | tf_op jit(solution)/shard_map/ppermute | solution.py:53
  380.2 3.6 collective-permute-start.19
  383.7 5.2 %collective-permute-start.18 = (f32[1,8,1024]{2,1,0:T(8,128)S(1)}, f32[1,8,1024]{2,1,0:T(8,128)S(1)}, u32[]{:S(2)}, u32[]{:S(2)}) collective-permute-start(f32[1,8,1024]{2,1,0:T(8,128)S(1)} %get-tuple-element.78), channel_id=1, source_target_pairs={{0,16},{1,17},{2,18},{3,19},{4,20},{5,21},{6,22},{7,23},{8,24},{9,... | collective-permute-start | bytes 98312 | tf_op jit(solution)/shard_map/ppermute | solution.py:53
  388.9 5.9 %collective-permute-start.17 = (f32[1,8,1024]{2,1,0:T(8,128)S(1)}, f32[1,8,1024]{2,1,0:T(8,128)S(1)}, u32[]{:S(2)}, u32[]{:S(2)}) collective-permute-start(f32[1,8,1024]{2,1,0:T(8,128)S(1)} %get-tuple-element.76), channel_id=1, source_target_pairs={{0,8},{1,9},{2,10},{3,11},{4,12},{5,13},{6,14},{7,15},{8,0},{9,1},... | collective-permute-start | bytes 98312 | tf_op jit(solution)/shard_map/ppermute | solution.py:53
  394.8 3.8 collective-permute-done.17
  398.6 4.3 %collective-permute-start.20 = (f32[1,8,1024]{2,1,0:T(8,128)S(1)}, f32[1,8,1024]{2,1,0:T(8,128)S(1)}, u32[]{:S(2)}, u32[]{:S(2)}) collective-permute-start(f32[1,8,1024]{2,1,0:T(8,128)S(1)} %add_add_fusion), channel_id=1, source_target_pairs={{0,384},{32,416},{64,448},{96,480},{128,256},{160,288},{192,320},{... | collective-permute-start | bytes 98312 | tf_op jit(solution)/shard_map/ppermute | solution.py:26
  403.0 3.8 collective-permute-start.21
  406.7 4.1 collective-permute-start.22
  413.5 4.5 %collective-permute-start.23 = (f32[2,2,1,8,1024]{4,3,1,0,2:T(8,128)S(1)}, f32[2,2,1,8,1024]{4,3,1,0,2:T(8,128)S(1)}, u32[]{:S(2)}, u32[]{:S(2)}) collective-permute-start(f32[2,2,1,8,1024]{4,3,1,0,2:T(8,128)S(1)} %bitcast.648), channel_id=1, source_target_pairs={{0,96},{32,64},{64,32},{96,0},{128,224},{160,192},{192,160},{224,1... | collective-permute-start | bytes 393224 | tf_op jit(solution)/shard_map/ppermute | solution.py:26
  419.9 2.9 collective-permute-start.25
  424.8 1.9 collective-permute-done.25
  (238 shorter events, 39.8 us)
Async XLA Ops:
  0.6 215.9 %copy-start = (bf16[8,512]{1,0:T(8,128)(2,1)S(1)}, bf16[8,512]{1,0:T(8,128)(2,1)}, u32[]{:S(2)}) copy-start(bf16[8,512]{1,0:T(8,128)(2,1)} %param.14) | copy-start | bytes 24580
  7.1 195.4 %all-to-all-start = ((bf16[32,128,1024]{1,2,0:T(8,128)(2,1)}), bf16[32,128,1024]{1,2,0:T(8,128)(2,1)}, u32[]{:S(2)}, u32[]{:S(2)}) async-start(bf16[32,128,1024]{1,2,0:T(8,128)(2,1)} %stack.134), calls=%async_computation | async-start | bytes 16777216 | tf_op jit(solution)/shard_map/all_to_all | solution.py:90
  219.7 24.2 %copy-start.2 = (bf16[4096,1024]{0,1:T(8,128)(2,1)S(1)}, bf16[4096,1024]{0,1:T(8,128)(2,1)}, u32[]{:S(2)}) copy-start(bf16[4096,1024]{0,1:T(8,128)(2,1)} %copy_bitcast_fusion) | copy-start | bytes 25165828
  226.9 19.4 %collective-permute-start = (f32[1,9,1024]{2,1,0:T(8,128)S(1)}, f32[1,9,1024]{2,1,0:T(8,128)S(1)}, u32[]{:S(2)}, u32[]{:S(2)}) collective-permute-start(f32[1,9,1024]{2,1,0:T(8,128)S(1)} %maximum_bitcast_fusion.1), channel_id=1, source_target_pairs={{0,384},{32,416},{64,448},{96,480},{128,256},{160,288},{192,320},{... | collective-permute-start | bytes 110600 | tf_op jit(solution)/shard_map/ppermute | solution.py:26
  237.6 10.7 %collective-permute-start.1 = (f32[1,9,1024]{2,1,0:T(8,128)S(1)}, f32[1,9,1024]{2,1,0:T(8,128)S(1)}, u32[]{:S(2)}, u32[]{:S(2)}) collective-permute-start(f32[1,9,1024]{2,1,0:T(8,128)S(1)} %maximum_bitcast_fusion.1), channel_id=1, source_target_pairs={{0,256},{32,288},{64,320},{96,352},{128,384},{160,416},{192,448},{... | collective-permute-start | bytes 110600 | tf_op jit(solution)/shard_map/ppermute | solution.py:26
  239.6 8.8 %collective-permute-start.2 = (f32[1,9,1024]{2,1,0:T(8,128)S(1)}, f32[1,9,1024]{2,1,0:T(8,128)S(1)}, u32[]{:S(2)}, u32[]{:S(2)}) collective-permute-start(f32[1,9,1024]{2,1,0:T(8,128)S(1)} %maximum_bitcast_fusion.1), channel_id=1, source_target_pairs={{0,128},{32,160},{64,192},{96,224},{128,0},{160,32},{192,64},{224,... | collective-permute-start | bytes 110600 | tf_op jit(solution)/shard_map/ppermute | solution.py:26
  248.5 14.1 %collective-permute-start.3 = (f32[2,2,1,9,1024]{4,3,1,0,2:T(8,128)S(1)}, f32[2,2,1,9,1024]{4,3,1,0,2:T(8,128)S(1)}, u32[]{:S(2)}, u32[]{:S(2)}) collective-permute-start(f32[2,2,1,9,1024]{4,3,1,0,2:T(8,128)S(1)} %bitcast.640), channel_id=1, source_target_pairs={{0,96},{32,64},{64,32},{96,0},{128,224},{160,192},{192,160},{224,1... | collective-permute-start | bytes 442376 | tf_op jit(solution)/shard_map/ppermute | solution.py:26
  252.6 10.0 %collective-permute-start.4 = (f32[2,2,1,9,1024]{4,3,1,0,2:T(8,128)S(1)}, f32[2,2,1,9,1024]{4,3,1,0,2:T(8,128)S(1)}, u32[]{:S(2)}, u32[]{:S(2)}) collective-permute-start(f32[2,2,1,9,1024]{4,3,1,0,2:T(8,128)S(1)} %bitcast.641), channel_id=1, source_target_pairs={{0,64},{32,96},{64,0},{96,32},{128,192},{160,224},{192,128},{224,1... | collective-permute-start | bytes 442376 | tf_op jit(solution)/shard_map/ppermute | solution.py:26
  255.0 9.0 %collective-permute-start.5 = (f32[2,2,1,9,1024]{4,3,1,0,2:T(8,128)S(1)}, f32[2,2,1,9,1024]{4,3,1,0,2:T(8,128)S(1)}, u32[]{:S(2)}, u32[]{:S(2)}) collective-permute-start(f32[2,2,1,9,1024]{4,3,1,0,2:T(8,128)S(1)} %bitcast.642), channel_id=1, source_target_pairs={{0,32},{32,0},{64,96},{96,64},{128,160},{160,128},{192,224},{224,1... | collective-permute-start | bytes 442376 | tf_op jit(solution)/shard_map/ppermute | solution.py:26
  264.5 41.1 %copy-start.24 = (f32[1,1,1024]{2,1,0:T(1,128)}, f32[1,1,1024]{2,1,0:T(1,128)S(1)}, u32[]{:S(2)}) copy-start(f32[1,1,1024]{2,1,0:T(1,128)S(1)} %get-tuple-element.35) | copy-start | bytes 12292
  264.5 41.1 %copy-start.26 = (f32[1,1,1024]{2,1,0:T(1,128)}, f32[1,1,1024]{2,1,0:T(1,128)S(1)}, u32[]{:S(2)}) copy-start(f32[1,1,1024]{2,1,0:T(1,128)S(1)} %get-tuple-element.36) | copy-start | bytes 12292
  265.3 20.4 %collective-permute-start.6 = (bf16[1,8,1024]{2,1,0:T(8,128)(2,1)S(1)}, bf16[1,8,1024]{2,1,0:T(8,128)(2,1)S(1)}, u32[]{:S(2)}, u32[]{:S(2)}) collective-permute-start(bf16[1,8,1024]{2,1,0:T(8,128)(2,1)S(1)} %get-tuple-element.23), channel_id=1, source_target_pairs={{0,24},{1,25},{2,26},{3,27},{4,28},{5,29},{6,30},{7,31},{8,16},{9,... | collective-permute-start | bytes 49160 | tf_op jit(solution)/shard_map/ppermute | solution.py:26
  270.3 15.4 %collective-permute-start.7 = (bf16[1,8,1024]{2,1,0:T(8,128)(2,1)S(1)}, bf16[1,8,1024]{2,1,0:T(8,128)(2,1)S(1)}, u32[]{:S(2)}, u32[]{:S(2)}) collective-permute-start(bf16[1,8,1024]{2,1,0:T(8,128)(2,1)S(1)} %get-tuple-element.23), channel_id=1, source_target_pairs={{0,16},{1,17},{2,18},{3,19},{4,20},{5,21},{6,22},{7,23},{8,24},{9,... | collective-permute-start | bytes 49160 | tf_op jit(solution)/shard_map/ppermute | solution.py:26
  275.5 10.2 %collective-permute-start.8 = (bf16[1,8,1024]{2,1,0:T(8,128)(2,1)S(1)}, bf16[1,8,1024]{2,1,0:T(8,128)(2,1)S(1)}, u32[]{:S(2)}, u32[]{:S(2)}) collective-permute-start(bf16[1,8,1024]{2,1,0:T(8,128)(2,1)S(1)} %get-tuple-element.23), channel_id=1, source_target_pairs={{0,8},{1,9},{2,10},{3,11},{4,12},{5,13},{6,14},{7,15},{8,0},{9,1},... | collective-permute-start | bytes 49160 | tf_op jit(solution)/shard_map/ppermute | solution.py:26
  285.8 19.9 %collective-permute-start.9 = (bf16[2,2,1,8,1024]{4,3,1,0,2:T(8,128)(2,1)S(1)}, bf16[2,2,1,8,1024]{4,3,1,0,2:T(8,128)(2,1)S(1)}, u32[]{:S(2)}, u32[]{:S(2)}) collective-permute-start(bf16[2,2,1,8,1024]{4,3,1,0,2:T(8,128)(2,1)S(1)} %bitcast.654), channel_id=1, source_target_pairs={{0,6},{1,7},{2,4},{3,5},{4,2},{5,3},{6,0},{7,1},{8,14},{9,15},{10,... | collective-permute-start | bytes 196616 | tf_op jit(solution)/shard_map/ppermute | solution.py:26
  295.7 9.9 %collective-permute-start.10 = (bf16[2,2,1,8,1024]{4,3,1,0,2:T(8,128)(2,1)S(1)}, bf16[2,2,1,8,1024]{4,3,1,0,2:T(8,128)(2,1)S(1)}, u32[]{:S(2)}, u32[]{:S(2)}) collective-permute-start(bf16[2,2,1,8,1024]{4,3,1,0,2:T(8,128)(2,1)S(1)} %bitcast.655), channel_id=1, source_target_pairs={{0,4},{1,5},{2,6},{3,7},{4,0},{5,1},{6,2},{7,3},{8,12},{9,13},{10,... | collective-permute-start | bytes 196616 | tf_op jit(solution)/shard_map/ppermute | solution.py:26
  297.7 8.0 %collective-permute-start.11 = (bf16[2,2,1,8,1024]{4,3,1,0,2:T(8,128)(2,1)S(1)}, bf16[2,2,1,8,1024]{4,3,1,0,2:T(8,128)(2,1)S(1)}, u32[]{:S(2)}, u32[]{:S(2)}) collective-permute-start(bf16[2,2,1,8,1024]{4,3,1,0,2:T(8,128)(2,1)S(1)} %bitcast.656), channel_id=1, source_target_pairs={{0,2},{1,3},{2,0},{3,1},{4,6},{5,7},{6,4},{7,5},{8,10},{9,11},{10,... | collective-permute-start | bytes 196616 | tf_op jit(solution)/shard_map/ppermute | solution.py:26
  305.7 6.7 %collective-permute-start.12 = (bf16[2,2,2,2,1,8,1024]{6,5,3,2,1,0,4:T(8,128)(2,1)S(1)}, bf16[2,2,2,2,1,8,1024]{6,5,3,2,1,0,4:T(8,128)(2,1)S(1)}, u32[]{:S(2)}, u32[]{:S(2)}) collective-permute-start(bf16[2,2,2,2,1,8,1024]{6,5,3,2,1,0,4:T(8,128)(2,1)S(1)} %bitcast.644), channel_id=1, source_target_pairs={{0,1},{1,0},{2,3},{3,2},{4,5},{5,4},{6,7},{7,6},{8,9},{9,8},{10,11... | collective-permute-start | bytes 786440 | tf_op jit(solution)/shard_map/ppermute | solution.py:26
  352.9 74.9 %copy-start.1 = (bf16[8,512]{1,0:T(8,128)(2,1)S(1)}, bf16[8,512]{1,0:T(8,128)(2,1)}, u32[]{:S(2)}) copy-start(bf16[8,512]{1,0:T(8,128)(2,1)} %param.14) | copy-start | bytes 24580
  354.7 68.1 %copy-start.10 = (bf16[128,4,4,128]{0,3,2,1:T(8,128)(2,1)S(1)}, bf16[128,4,4,128]{0,3,2,1:T(8,128)(2,1)}, u32[]{:S(2)}) copy-start(bf16[128,4,4,128]{0,3,2,1:T(8,128)(2,1)} %get-tuple-element.104) | copy-start | bytes 1572868
  354.7 72.2 %copy-start.25 = (f32[1,1,1024]{2,1,0:T(1,128)S(1)}, f32[1,1,1024]{2,1,0:T(1,128)}, u32[]{:S(2)}) copy-start(f32[1,1,1024]{2,1,0:T(1,128)} %copy-done.24) | copy-start | bytes 12292
  354.7 72.2 %copy-start.27 = (f32[1,1,1024]{2,1,0:T(1,128)S(1)}, f32[1,1,1024]{2,1,0:T(1,128)}, u32[]{:S(2)}) copy-start(f32[1,1,1024]{2,1,0:T(1,128)} %copy-done.26) | copy-start | bytes 12292
  354.7 72.2 %copy-start.29 = (f32[1,1,1024]{2,1,0:T(1,128)S(1)}, f32[1,1,1024]{2,1,0:T(1,128)}, u32[]{:S(2)}) copy-start(f32[1,1,1024]{2,1,0:T(1,128)} %copy-done.28) | copy-start | bytes 12292
  354.7 72.2 %copy-start.31 = (f32[1,1,1024]{2,1,0:T(1,128)S(1)}, f32[1,1,1024]{2,1,0:T(1,128)}, u32[]{:S(2)}) copy-start(f32[1,1,1024]{2,1,0:T(1,128)} %copy-done.30) | copy-start | bytes 12292
  354.8 72.2 %copy-start.33 = (f32[1,1,1024]{2,1,0:T(1,128)S(1)}, f32[1,1,1024]{2,1,0:T(1,128)}, u32[]{:S(2)}) copy-start(f32[1,1,1024]{2,1,0:T(1,128)} %copy-done.32) | copy-start | bytes 12292
  354.8 72.2 %copy-start.35 = (f32[1,1,1024]{2,1,0:T(1,128)S(1)}, f32[1,1,1024]{2,1,0:T(1,128)}, u32[]{:S(2)}) copy-start(f32[1,1,1024]{2,1,0:T(1,128)} %copy-done.34) | copy-start | bytes 12292
  354.8 72.2 %copy-start.37 = (f32[1,1,1024]{2,1,0:T(1,128)S(1)}, f32[1,1,1024]{2,1,0:T(1,128)}, u32[]{:S(2)}) copy-start(f32[1,1,1024]{2,1,0:T(1,128)} %copy-done.36) | copy-start | bytes 12292
  354.8 72.2 %copy-start.39 = (f32[1,1,1024]{2,1,0:T(1,128)S(1)}, f32[1,1,1024]{2,1,0:T(1,128)}, u32[]{:S(2)}) copy-start(f32[1,1,1024]{2,1,0:T(1,128)} %copy-done.38) | copy-start | bytes 12292
  354.8 72.2 %copy-start.41 = (f32[1,1,1024]{2,1,0:T(1,128)S(1)}, f32[1,1,1024]{2,1,0:T(1,128)}, u32[]{:S(2)}) copy-start(f32[1,1,1024]{2,1,0:T(1,128)} %copy-done.40) | copy-start | bytes 12292
  354.8 72.2 %copy-start.43 = (f32[1,1,1024]{2,1,0:T(1,128)S(1)}, f32[1,1,1024]{2,1,0:T(1,128)}, u32[]{:S(2)}) copy-start(f32[1,1,1024]{2,1,0:T(1,128)} %copy-done.42) | copy-start | bytes 12292
  354.8 72.2 %copy-start.45 = (f32[1,1,1024]{2,1,0:T(1,128)S(1)}, f32[1,1,1024]{2,1,0:T(1,128)}, u32[]{:S(2)}) copy-start(f32[1,1,1024]{2,1,0:T(1,128)} %copy-done.44) | copy-start | bytes 12292
  354.8 72.2 %copy-start.47 = (f32[1,1,1024]{2,1,0:T(1,128)S(1)}, f32[1,1,1024]{2,1,0:T(1,128)}, u32[]{:S(2)}) copy-start(f32[1,1,1024]{2,1,0:T(1,128)} %copy-done.46) | copy-start | bytes 12292
  354.8 72.2 %copy-start.49 = (f32[1,1,1024]{2,1,0:T(1,128)S(1)}, f32[1,1,1024]{2,1,0:T(1,128)}, u32[]{:S(2)}) copy-start(f32[1,1,1024]{2,1,0:T(1,128)} %copy-done.48) | copy-start | bytes 12292
  354.8 72.2 %copy-start.51 = (f32[1,1,1024]{2,1,0:T(1,128)S(1)}, f32[1,1,1024]{2,1,0:T(1,128)}, u32[]{:S(2)}) copy-start(f32[1,1,1024]{2,1,0:T(1,128)} %copy-done.50) | copy-start | bytes 12292
  354.9 72.2 %copy-start.53 = (f32[1,1,1024]{2,1,0:T(1,128)S(1)}, f32[1,1,1024]{2,1,0:T(1,128)}, u32[]{:S(2)}) copy-start(f32[1,1,1024]{2,1,0:T(1,128)} %copy-done.52) | copy-start | bytes 12292
  358.2 3.9 collective-permute-start.13
  362.2 10.2 %collective-permute-start.16 = (f32[4,8,1024]{2,1,0:T(8,128)S(1)}, f32[4,8,1024]{2,1,0:T(8,128)S(1)}, u32[]{:S(2)}, u32[]{:S(2)}) collective-permute-start(f32[4,8,1024]{2,1,0:T(8,128)S(1)} %get-tuple-element.59), channel_id=1, source_target_pairs={{0,6},{1,7},{2,4},{3,5},{4,2},{5,3},{6,0},{7,1},{8,14},{9,15},{10,... | collective-permute-start | bytes 393224 | tf_op jit(solution)/shard_map/ppermute | solution.py:53
  368.0 11.4 %collective-permute-start.15 = (f32[4,8,1024]{2,1,0:T(8,128)S(1)}, f32[4,8,1024]{2,1,0:T(8,128)S(1)}, u32[]{:S(2)}, u32[]{:S(2)}) collective-permute-start(f32[4,8,1024]{2,1,0:T(8,128)S(1)} %get-tuple-element.60), channel_id=1, source_target_pairs={{0,4},{1,5},{2,6},{3,7},{4,0},{5,1},{6,2},{7,3},{8,12},{9,13},{10,... | collective-permute-start | bytes 393224 | tf_op jit(solution)/shard_map/ppermute | solution.py:53
  369.9 10.2 %collective-permute-start.14 = (f32[4,8,1024]{2,1,0:T(8,128)S(1)}, f32[4,8,1024]{2,1,0:T(8,128)S(1)}, u32[]{:S(2)}, u32[]{:S(2)}) collective-permute-start(f32[4,8,1024]{2,1,0:T(8,128)S(1)} %get-tuple-element.58), channel_id=1, source_target_pairs={{0,2},{1,3},{2,0},{3,1},{4,6},{5,7},{6,4},{7,5},{8,10},{9,11},{10,... | collective-permute-start | bytes 393224 | tf_op jit(solution)/shard_map/ppermute | solution.py:53
  380.2 14.7 %collective-permute-start.19 = (f32[1,8,1024]{2,1,0:T(8,128)S(1)}, f32[1,8,1024]{2,1,0:T(8,128)S(1)}, u32[]{:S(2)}, u32[]{:S(2)}) collective-permute-start(f32[1,8,1024]{2,1,0:T(8,128)S(1)} %get-tuple-element.77), channel_id=1, source_target_pairs={{0,24},{1,25},{2,26},{3,27},{4,28},{5,29},{6,30},{7,31},{8,16},{9,... | collective-permute-start | bytes 98312 | tf_op jit(solution)/shard_map/ppermute | solution.py:53
  383.7 11.1 %collective-permute-start.18 = (f32[1,8,1024]{2,1,0:T(8,128)S(1)}, f32[1,8,1024]{2,1,0:T(8,128)S(1)}, u32[]{:S(2)}, u32[]{:S(2)}) collective-permute-start(f32[1,8,1024]{2,1,0:T(8,128)S(1)} %get-tuple-element.78), channel_id=1, source_target_pairs={{0,16},{1,17},{2,18},{3,19},{4,20},{5,21},{6,22},{7,23},{8,24},{9,... | collective-permute-start | bytes 98312 | tf_op jit(solution)/shard_map/ppermute | solution.py:53
  388.9 9.7 %collective-permute-start.17 = (f32[1,8,1024]{2,1,0:T(8,128)S(1)}, f32[1,8,1024]{2,1,0:T(8,128)S(1)}, u32[]{:S(2)}, u32[]{:S(2)}) collective-permute-start(f32[1,8,1024]{2,1,0:T(8,128)S(1)} %get-tuple-element.76), channel_id=1, source_target_pairs={{0,8},{1,9},{2,10},{3,11},{4,12},{5,13},{6,14},{7,15},{8,0},{9,1},... | collective-permute-start | bytes 98312 | tf_op jit(solution)/shard_map/ppermute | solution.py:53
  398.6 12.2 %collective-permute-start.20 = (f32[1,8,1024]{2,1,0:T(8,128)S(1)}, f32[1,8,1024]{2,1,0:T(8,128)S(1)}, u32[]{:S(2)}, u32[]{:S(2)}) collective-permute-start(f32[1,8,1024]{2,1,0:T(8,128)S(1)} %add_add_fusion), channel_id=1, source_target_pairs={{0,384},{32,416},{64,448},{96,480},{128,256},{160,288},{192,320},{... | collective-permute-start | bytes 98312 | tf_op jit(solution)/shard_map/ppermute | solution.py:26
  403.0 9.7 %collective-permute-start.21 = (f32[1,8,1024]{2,1,0:T(8,128)S(1)}, f32[1,8,1024]{2,1,0:T(8,128)S(1)}, u32[]{:S(2)}, u32[]{:S(2)}) collective-permute-start(f32[1,8,1024]{2,1,0:T(8,128)S(1)} %add_add_fusion), channel_id=1, source_target_pairs={{0,256},{32,288},{64,320},{96,352},{128,384},{160,416},{192,448},{... | collective-permute-start | bytes 98312 | tf_op jit(solution)/shard_map/ppermute | solution.py:26
  406.7 6.7 %collective-permute-start.22 = (f32[1,8,1024]{2,1,0:T(8,128)S(1)}, f32[1,8,1024]{2,1,0:T(8,128)S(1)}, u32[]{:S(2)}, u32[]{:S(2)}) collective-permute-start(f32[1,8,1024]{2,1,0:T(8,128)S(1)} %add_add_fusion), channel_id=1, source_target_pairs={{0,128},{32,160},{64,192},{96,224},{128,0},{160,32},{192,64},{224,... | collective-permute-start | bytes 98312 | tf_op jit(solution)/shard_map/ppermute | solution.py:26
  413.5 10.4 %collective-permute-start.23 = (f32[2,2,1,8,1024]{4,3,1,0,2:T(8,128)S(1)}, f32[2,2,1,8,1024]{4,3,1,0,2:T(8,128)S(1)}, u32[]{:S(2)}, u32[]{:S(2)}) collective-permute-start(f32[2,2,1,8,1024]{4,3,1,0,2:T(8,128)S(1)} %bitcast.648), channel_id=1, source_target_pairs={{0,96},{32,64},{64,32},{96,0},{128,224},{160,192},{192,160},{224,1... | collective-permute-start | bytes 393224 | tf_op jit(solution)/shard_map/ppermute | solution.py:26
  417.9 6.9 %collective-permute-start.24 = (f32[2,2,1,8,1024]{4,3,1,0,2:T(8,128)S(1)}, f32[2,2,1,8,1024]{4,3,1,0,2:T(8,128)S(1)}, u32[]{:S(2)}, u32[]{:S(2)}) collective-permute-start(f32[2,2,1,8,1024]{4,3,1,0,2:T(8,128)S(1)} %bitcast.649), channel_id=1, source_target_pairs={{0,64},{32,96},{64,0},{96,32},{128,192},{160,224},{192,128},{224,1... | collective-permute-start | bytes 393224 | tf_op jit(solution)/shard_map/ppermute | solution.py:26
  419.9 6.9 %collective-permute-start.25 = (f32[2,2,1,8,1024]{4,3,1,0,2:T(8,128)S(1)}, f32[2,2,1,8,1024]{4,3,1,0,2:T(8,128)S(1)}, u32[]{:S(2)}, u32[]{:S(2)}) collective-permute-start(f32[2,2,1,8,1024]{4,3,1,0,2:T(8,128)S(1)} %bitcast.650), channel_id=1, source_target_pairs={{0,32},{32,0},{64,96},{96,64},{128,160},{160,128},{192,224},{224,1... | collective-permute-start | bytes 393224 | tf_op jit(solution)/shard_map/ppermute | solution.py:26
  (51 other events, 513.7 us)
